TPU v7x, 32 devices: a whole 2x2x4 slice. The times are simulated.
32 devices in a mesh: section: 2 (over x), tm: 4 (over z), space: 4 (over y, core).
Axes of the slice: x: 2, y: 2, z: 4, core: 2. Of those that a mesh axis runs over, the one named last changes fastest.
Arguments:
- video: bfloat16 [2, 8, 16, 512, 128], P('section', 'tm', 'space'), may hold values from -6 to 6
- weights: bfloat16 [2, 9, 384, 128], P('section'), may hold values from -0.109375 to 0.109375
Outputs:
- decoded: bfloat16 [2, 8, 16, 512, 128], P('section', 'tm', 'space')
All inputs are finite; a program needn't handle non-finite values.
Results may differ from a plain program's by a relative error of at most 0.0095.
Values may be sent and summed in bfloat16 or wider, within the bound.
No kernel may reach another device: no remote copies, remote signals or barrier semaphores. Data moves between devices by JAX's collectives and lax.ppermute only.
A program may use at most 128 MiB of HBM per device.

v0:
```python
import jax
import jax.numpy as jnp
from jax import lax
from jax.sharding import PartitionSpec as P


def from_behind(block, axis, distance):
    devices = range(lax.axis_size(axis))
    route = [(i - distance, i) for i in devices if i - distance in devices]
    return lax.ppermute(block, axis, route)


def padded_2(cells, sides, width):
    for axis, dim in sides:
        count = lax.axis_size(axis)
        ends = count - 1
        head = lax.slice_in_dim(cells, 0, width, axis=dim)
        tail = lax.slice_in_dim(cells, cells.shape[dim] - width, cells.shape[dim], axis=dim)
        cells = jnp.concatenate(
            [
                lax.ppermute(tail, axis, [(i, (i + 1) % count) for i in range(ends)]),
                cells,
                lax.ppermute(head, axis, [((i + 1) % count, i) for i in range(ends)]),
            ],
            axis=dim,
        )
    return cells


def conv_block(clip, taps):
    frames, rows, width, chans = clip.shape
    act = jax.nn.silu(clip.astype(jnp.float32)).astype(jnp.bfloat16)
    carried = from_behind(act, "tm", 1)
    extended = jnp.concatenate([carried, act], axis=0)
    padded = padded_2(extended, (("space", 1),), 1)
    padded = jnp.pad(padded, ((0, 0), (0, 0), (1, 1), (0, 0)))
    joined = jnp.concatenate(
        [padded[:, :, 0:width], padded[:, :, 1 : width + 1], padded[:, :, 2 : width + 2]], axis=-1
    )
    total = jnp.zeros((frames * rows * width, chans), jnp.float32)
    for time_tap in range(3):
        for row_tap in range(3):
            slab = joined[time_tap : time_tap + frames, row_tap : row_tap + rows]
            total = total + jnp.dot(
                slab.reshape(-1, 3 * chans),
                taps[time_tap * 3 + row_tap],
                preferred_element_type=jnp.float32,
            )
    return (clip.astype(jnp.float32) + total.reshape(clip.shape)).astype(jnp.bfloat16)


def body(video, weights):
    all_taps = lax.all_gather(weights, "section", axis=0, tiled=True)
    first_taps = all_taps[0]
    second_taps = all_taps[1]
    index = 0
    hiddens = [conv_block(video[index], first_taps)]
    index = 0
    finished = [conv_block(hiddens[index], second_taps)]
    return jnp.stack(finished, axis=0)


def solution(mesh):
    return jax.shard_map(
        body,
        mesh=mesh,
        in_specs=(P("section", "tm", "space", None, None), P("section", None, None, None)),
        out_specs=P("section", "tm", "space", None, None),
        check_vma=False,
    )
```

profile of v0, /device:TPU:9, one launch (start us, length us, event | category | flops | bytes accessed | tf_op | source)
XLA Modules:
  0.0 177.2 jit_solution(865191045750303736)
XLA Ops:
  6.5 1.8 %fusion.24 = bf16[2,4,512,128]{3,2,1,0:T(8,128)(2,1)S(1)} fusion(bf16[1,2,4,512,128]{4,3,2,1,0:T(8,128)(2,1)} %param.2), kind=kLoop, calls=%fused_computation.39 | loop fusion | flops 3145728 | bytes 2097152 | tf_op jit(solution)/shard_map/convert_element_type | solution.py:32
  8.3 3.2 %collective-permute-start = (bf16[2,4,512,128]{3,2,1,0:T(8,128)(2,1)S(1)}, bf16[2,4,512,128]{3,2,1,0:T(8,128)(2,1)S(1)}, u32[]{:S(2)}, u32[]{:S(2)}) collective-permute-start(bf16[2,4,512,128]{3,2,1,0:T(8,128)(2,1)S(1)} %fusion.24), channel_id=1, source_target_pairs={{0,4},{4,8},{8,12},{1,5},{5,9},{9,13},{2,6},{6,10},{10,14},{3,7},{... | collective-permute-start | bytes 3145736 | tf_op jit(solution)/shard_map/ppermute | solution.py:10
  11.5 22.7 %collective-permute-done = bf16[2,4,512,128]{3,2,1,0:T(8,128)(2,1)S(1)} collective-permute-done((bf16[2,4,512,128]{3,2,1,0:T(8,128)(2,1)S(1)}, bf16[2,4,512,128]{3,2,1,0:T(8,128)(2,1)S(1)}, u32[]{:S(2)}, u32[]{:S(2)}) %collective-permute-start) | collective-permute-done | bytes 1048608 | tf_op jit(solution)/shard_map/ppermute | solution.py:10
  34.2 1.1 pad_maximum_fusion.5
  35.3 4.6 %collective-permute-start.1 = (bf16[4,1,512,128]{3,2,1,0:T(8,128)(2,1)}, bf16[4,1,512,128]{3,2,1,0:T(8,128)(2,1)S(1)}, u32[]{:S(2)}, u32[]{:S(2)}) collective-permute-start(bf16[4,1,512,128]{3,2,1,0:T(8,128)(2,1)} %get-tuple-element.29), channel_id=1, source_target_pairs={{0,1},{1,2},{2,3},{4,5},{5,6},{6,7},{8,9},{9,10},{10,11},{12,13},{... | collective-permute-start | bytes 1572872 | tf_op jit(solution)/shard_map/ppermute | solution.py:21
  39.9 1.9 %collective-permute-start.2 = (bf16[4,1,512,128]{3,2,1,0:T(8,128)(2,1)}, bf16[4,1,512,128]{3,2,1,0:T(8,128)(2,1)S(1)}, u32[]{:S(2)}, u32[]{:S(2)}) collective-permute-start(bf16[4,1,512,128]{3,2,1,0:T(8,128)(2,1)} %get-tuple-element.30), channel_id=1, source_target_pairs={{1,0},{2,1},{3,2},{5,4},{6,5},{7,6},{9,8},{10,9},{11,10},{13,12},{... | collective-permute-start | bytes 1572872 | tf_op jit(solution)/shard_map/ppermute | solution.py:23
  41.8 0.0 all-gather.2.cloned.1.call-update
  41.8 4.5 %collective-permute-done.1 = bf16[4,1,512,128]{3,2,1,0:T(8,128)(2,1)S(1)} collective-permute-done((bf16[4,1,512,128]{3,2,1,0:T(8,128)(2,1)}, bf16[4,1,512,128]{3,2,1,0:T(8,128)(2,1)S(1)}, u32[]{:S(2)}, u32[]{:S(2)}) %collective-permute-start.1) | collective-permute-done | bytes 524320 | tf_op jit(solution)/shard_map/ppermute | solution.py:21
  46.3 4.3 %collective-permute-done.2 = bf16[4,1,512,128]{3,2,1,0:T(8,128)(2,1)S(1)} collective-permute-done((bf16[4,1,512,128]{3,2,1,0:T(8,128)(2,1)}, bf16[4,1,512,128]{3,2,1,0:T(8,128)(2,1)S(1)}, u32[]{:S(2)}, u32[]{:S(2)}) %collective-permute-start.2) | collective-permute-done | bytes 524320 | tf_op jit(solution)/shard_map/ppermute | solution.py:23
  50.6 1.9 %select_maximum_fusion.3 = bf16[4,6,514,128]{3,2,1,0:T(8,128)(2,1)S(1)} fusion(bf16[4,1,512,128]{3,2,1,0:T(8,128)(2,1)S(1)} %collective-permute-done.2, bf16[4,1,512,128]{3,2,1,0:T(8,128)(2,1)S(1)} %collective-permute-done.1, bf16[2,4,512,128]{3,2,1,0:T(8,128)(2,1)S(1)} %fusion.24, bf16[2,4,512,128]{3,2,1,0:T(8,128)(2,1)S(1)} %collective-permute-done), kind=kLoop, calls=%fused_computation.24 | loop fusion | flops 23685120 | bytes 6303744 | tf_op jit(solution)/shard_map/concatenate | solution.py:19
  52.5 2.3 %fusion.50 = (bf16[4,6,512,128]{3,2,1,0:T(8,128)(2,1)S(1)}, bf16[4,6,512,128]{3,2,1,0:T(8,128)(2,1)S(1)}) fusion(bf16[4,6,514,128]{3,2,1,0:T(8,128)(2,1)S(1)} %select_maximum_fusion.3), kind=kLoop, calls=%fused_computation.88 | loop fusion | bytes 12582912 | tf_op jit(solution)/shard_map/slice | solution.py:38
  54.8 1.7 pad_maximum_fusion
  56.5 9.3 %fusion.48 = (bf16[2,4,512,384]{3,2,1,0:T(8,128)(2,1)}, bf16[2,4,512,384]{3,2,1,0:T(8,128)(2,1)}, bf16[2,4,512,384]{3,2,1,0:T(8,128)(2,1)}, bf16[2,4,512,384]{3,...) fusion(bf16[4,6,512,384]{3,2,1,0:T(8,128)(2,1)S(1)} %pad_maximu, ...), kind=kLoop, calls=%fused_computation.86 | loop fusion | bytes 56623104 | tf_op jit(solution)/shard_map/slice | solution.py:43
  65.8 6.7 %all-gather.2.cloned.1.call-done = bf16[2,9,384,128]{3,2,1,0:T(8,128)(2,1)} async-done(((bf16[1,9,384,128]{3,2,1,0:T(8,128)(2,1)}), bf16[2,9,384,128]{3,2,1,0:T(8,128)(2,1)}) %all-gather.2.cloned.1.call-update) | async-done | bytes 1769488 | tf_op jit(solution)/shard_map/all_gather | solution.py:53
  72.5 3.0 %fusion.39 = f32[4096,128]{1,0:T(8,128)S(1)} fusion(bf16[4096,384]{1,0:T(8,128)(2,1)} %bitcast.128, bf16[2,9,384,128]{3,2,1,0:T(8,128)(2,1)} %all-gather.2.cloned.1.call-done), kind=kOutput, calls=%fused_computation.69 | convolution fusion | flops 402653184 | bytes 5341184 | tf_op jit(solution)/shard_map/dot_general | solution.py:44
  75.6 2.0 %fusion.40 = f32[4096,128]{1,0:T(8,128)S(1)} fusion(bf16[4096,384]{1,0:T(8,128)(2,1)S(1)} %bitcast.126, bf16[2,9,384,128]{3,2,1,0:T(8,128)(2,1)} %all-gather.2.cloned.1.call-done), kind=kOutput, calls=%fused_computation.71 | convolution fusion | flops 402653184 | bytes 5341184 | tf_op jit(solution)/shard_map/dot_general | solution.py:44
  77.6 2.0 %fusion.41 = f32[4096,128]{1,0:T(8,128)S(1)} fusion(bf16[4096,384]{1,0:T(8,128)(2,1)S(1)} %bitcast.124, bf16[2,9,384,128]{3,2,1,0:T(8,128)(2,1)} %all-gather.2.cloned.1.call-done), kind=kOutput, calls=%fused_computation.73 | convolution fusion | flops 402653184 | bytes 5341184 | tf_op jit(solution)/shard_map/dot_general | solution.py:44
  79.7 2.0 %fusion.42 = f32[4096,128]{1,0:T(8,128)S(1)} fusion(bf16[4096,384]{1,0:T(8,128)(2,1)S(1)} %bitcast.122, bf16[2,9,384,128]{3,2,1,0:T(8,128)(2,1)} %all-gather.2.cloned.1.call-done), kind=kOutput, calls=%fused_computation.75 | convolution fusion | flops 402653184 | bytes 5341184 | tf_op jit(solution)/shard_map/dot_general | solution.py:44
  81.7 2.0 %fusion.43 = f32[4096,128]{1,0:T(8,128)S(1)} fusion(bf16[4096,384]{1,0:T(8,128)(2,1)S(1)} %bitcast.120, bf16[2,9,384,128]{3,2,1,0:T(8,128)(2,1)} %all-gather.2.cloned.1.call-done), kind=kOutput, calls=%fused_computation.77 | convolution fusion | flops 402653184 | bytes 5341184 | tf_op jit(solution)/shard_map/dot_general | solution.py:44
  83.7 0.0 copy-done.1
  83.8 0.0 copy-start
  83.8 2.0 %fusion.44 = f32[4096,128]{1,0:T(8,128)S(1)} fusion(bf16[4096,384]{1,0:T(8,128)(2,1)S(1)} %bitcast.119, bf16[2,9,384,128]{3,2,1,0:T(8,128)(2,1)} %all-gather.2.cloned.1.call-done), kind=kOutput, calls=%fused_computation.79 | convolution fusion | flops 402653184 | bytes 5341184 | tf_op jit(solution)/shard_map/dot_general | solution.py:44
  85.8 1.9 %fusion.45 = f32[4096,128]{1,0:T(8,128)S(1)} fusion(bf16[4096,384]{1,0:T(8,128)(2,1)S(1)} %bitcast.118, bf16[2,9,384,128]{3,2,1,0:T(8,128)(2,1)} %all-gather.2.cloned.1.call-done), kind=kOutput, calls=%fused_computation.81 | convolution fusion | flops 402653184 | bytes 5341184 | tf_op jit(solution)/shard_map/dot_general | solution.py:44
  87.7 2.0 %fusion.46 = f32[4096,128]{1,0:T(8,128)S(1)} fusion(bf16[4096,384]{1,0:T(8,128)(2,1)S(1)} %bitcast.117, bf16[2,9,384,128]{3,2,1,0:T(8,128)(2,1)} %all-gather.2.cloned.1.call-done), kind=kOutput, calls=%fused_computation.83 | convolution fusion | flops 402653184 | bytes 5341184 | tf_op jit(solution)/shard_map/dot_general | solution.py:44
  89.7 0.0 copy-start.14
  89.7 2.8 %fusion.14 = f32[4096,128]{1,0:T(8,128)S(1)} fusion(f32[4096,128]{1,0:T(8,128)S(1)} %fusion.39, f32[4096,128]{1,0:T(8,128)S(1)} %fusion.40, f32[4096,128]{1,0:T(8,128)S(1)} %fusion.41, f32[4096,128]{1,0:T(8,128)S(1)} %fusion.42, f32[4096,128]{1,0:T(8,128)S(1)} %fusion.43, f32[4096,128]{1,0:T(8,128)S(1)} %fusion.44, f32[4096,128]{1,0:T(8,128)S(1)} %fusion.45, ...), kind=kOutput, calls=%fused_computation.20 | convolution fusion | flops 406847488 | bytes 22118400 | tf_op jit(solution)/shard_map/dot_general | solution.py:44
  92.6 0.6 fusion.30
  93.1 3.1 %collective-permute-start.3 = (bf16[2,4,512,128]{3,2,1,0:T(8,128)(2,1)S(1)}, bf16[2,4,512,128]{3,2,1,0:T(8,128)(2,1)S(1)}, u32[]{:S(2)}, u32[]{:S(2)}) collective-permute-start(bf16[2,4,512,128]{3,2,1,0:T(8,128)(2,1)S(1)} %fusion.30), channel_id=1, source_target_pairs={{0,4},{4,8},{8,12},{1,5},{5,9},{9,13},{2,6},{6,10},{10,14},{3,7},{... | collective-permute-start | bytes 3145736 | tf_op jit(solution)/shard_map/ppermute | solution.py:10
  96.3 22.8 %collective-permute-done.3 = bf16[2,4,512,128]{3,2,1,0:T(8,128)(2,1)S(1)} collective-permute-done((bf16[2,4,512,128]{3,2,1,0:T(8,128)(2,1)S(1)}, bf16[2,4,512,128]{3,2,1,0:T(8,128)(2,1)S(1)}, u32[]{:S(2)}, u32[]{:S(2)}) %collective-permute-start.3) | collective-permute-done | bytes 1048608 | tf_op jit(solution)/shard_map/ppermute | solution.py:10
  119.1 0.1 pad_maximum_fusion.3
  119.2 4.5 %collective-permute-start.4 = (bf16[4,1,512,128]{3,2,1,0:T(8,128)(2,1)S(1)}, bf16[4,1,512,128]{3,2,1,0:T(8,128)(2,1)S(1)}, u32[]{:S(2)}, u32[]{:S(2)}) collective-permute-start(bf16[4,1,512,128]{3,2,1,0:T(8,128)(2,1)S(1)} %get-tuple-element.27), channel_id=1, source_target_pairs={{0,1},{1,2},{2,3},{4,5},{5,6},{6,7},{8,9},{9,10},{10,11},{12,13},{... | collective-permute-start | bytes 1572872 | tf_op jit(solution)/shard_map/ppermute | solution.py:21
  123.7 1.9 %collective-permute-start.5 = (bf16[4,1,512,128]{3,2,1,0:T(8,128)(2,1)S(1)}, bf16[4,1,512,128]{3,2,1,0:T(8,128)(2,1)S(1)}, u32[]{:S(2)}, u32[]{:S(2)}) collective-permute-start(bf16[4,1,512,128]{3,2,1,0:T(8,128)(2,1)S(1)} %get-tuple-element.28), channel_id=1, source_target_pairs={{1,0},{2,1},{3,2},{5,4},{6,5},{7,6},{9,8},{10,9},{11,10},{13,12},{... | collective-permute-start | bytes 1572872 | tf_op jit(solution)/shard_map/ppermute | solution.py:23
  125.6 4.2 %collective-permute-done.4 = bf16[4,1,512,128]{3,2,1,0:T(8,128)(2,1)S(1)} collective-permute-done((bf16[4,1,512,128]{3,2,1,0:T(8,128)(2,1)S(1)}, bf16[4,1,512,128]{3,2,1,0:T(8,128)(2,1)S(1)}, u32[]{:S(2)}, u32[]{:S(2)}) %collective-permute-start.4) | collective-permute-done | bytes 524320 | tf_op jit(solution)/shard_map/ppermute | solution.py:21
  129.8 4.4 %collective-permute-done.5 = bf16[4,1,512,128]{3,2,1,0:T(8,128)(2,1)S(1)} collective-permute-done((bf16[4,1,512,128]{3,2,1,0:T(8,128)(2,1)S(1)}, bf16[4,1,512,128]{3,2,1,0:T(8,128)(2,1)S(1)}, u32[]{:S(2)}, u32[]{:S(2)}) %collective-permute-start.5) | collective-permute-done | bytes 524320 | tf_op jit(solution)/shard_map/ppermute | solution.py:23
  134.2 1.9 %select_maximum_fusion = bf16[4,6,514,128]{3,2,1,0:T(8,128)(2,1)S(1)} fusion(bf16[4,1,512,128]{3,2,1,0:T(8,128)(2,1)S(1)} %collective-permute-done.5, bf16[4,1,512,128]{3,2,1,0:T(8,128)(2,1)S(1)} %collective-permute-done.4, bf16[2,4,512,128]{3,2,1,0:T(8,128)(2,1)S(1)} %fusion.30, bf16[2,4,512,128]{3,2,1,0:T(8,128)(2,1)S(1)} %collective-permute-done.3), kind=kLoop, calls=%fused_computation.21 | loop fusion | flops 23685120 | bytes 6303744 | tf_op jit(solution)/shard_map/concatenate | solution.py:19
  136.1 2.3 %fusion.49 = (bf16[4,6,512,128]{3,2,1,0:T(8,128)(2,1)S(1)}, bf16[4,6,512,128]{3,2,1,0:T(8,128)(2,1)S(1)}) fusion(bf16[4,6,514,128]{3,2,1,0:T(8,128)(2,1)S(1)} %select_maximum_fusion), kind=kLoop, calls=%fused_computation.87 | loop fusion | bytes 12582912 | tf_op jit(solution)/shard_map/slice | solution.py:38
  138.4 1.7 pad_maximum_fusion.1
  140.1 9.3 %fusion.47 = (bf16[2,4,512,384]{3,2,1,0:T(8,128)(2,1)}, bf16[2,4,512,384]{3,2,1,0:T(8,128)(2,1)}, bf16[2,4,512,384]{3,2,1,0:T(8,128)(2,1)}, bf16[2,4,512,384]{3,...) fusion(bf16[4,6,512,384]{3,2,1,0:T(8,128)(2,1)S(1)} %pad_maximu, ...), kind=kLoop, calls=%fused_computation.85 | loop fusion | bytes 56623104 | tf_op jit(solution)/shard_map/slice | solution.py:43
  149.5 3.0 %fusion.31 = f32[4096,128]{1,0:T(8,128)S(1)} fusion(bf16[4096,384]{1,0:T(8,128)(2,1)} %bitcast.132, bf16[2,9,384,128]{3,2,1,0:T(8,128)(2,1)} %all-gather.2.cloned.1.call-done), kind=kOutput, calls=%fused_computation.52 | convolution fusion | flops 402653184 | bytes 5341184 | tf_op jit(solution)/shard_map/dot_general | solution.py:44
  152.5 2.0 %fusion.32 = f32[4096,128]{1,0:T(8,128)S(1)} fusion(bf16[4096,384]{1,0:T(8,128)(2,1)S(1)} %bitcast.131, bf16[2,9,384,128]{3,2,1,0:T(8,128)(2,1)} %all-gather.2.cloned.1.call-done), kind=kOutput, calls=%fused_computation.54 | convolution fusion | flops 402653184 | bytes 5341184 | tf_op jit(solution)/shard_map/dot_general | solution.py:44
  154.6 2.0 %fusion.33 = f32[4096,128]{1,0:T(8,128)S(1)} fusion(bf16[4096,384]{1,0:T(8,128)(2,1)S(1)} %bitcast.130, bf16[2,9,384,128]{3,2,1,0:T(8,128)(2,1)} %all-gather.2.cloned.1.call-done), kind=kOutput, calls=%fused_computation.56 | convolution fusion | flops 402653184 | bytes 5341184 | tf_op jit(solution)/shard_map/dot_general | solution.py:44
  156.6 2.0 %fusion.34 = f32[4096,128]{1,0:T(8,128)S(1)} fusion(bf16[4096,384]{1,0:T(8,128)(2,1)S(1)} %bitcast.129, bf16[2,9,384,128]{3,2,1,0:T(8,128)(2,1)} %all-gather.2.cloned.1.call-done), kind=kOutput, calls=%fused_computation.58 | convolution fusion | flops 402653184 | bytes 5341184 | tf_op jit(solution)/shard_map/dot_general | solution.py:44
  158.7 2.0 %fusion.35 = f32[4096,128]{1,0:T(8,128)S(1)} fusion(bf16[4096,384]{1,0:T(8,128)(2,1)S(1)} %bitcast.127, bf16[2,9,384,128]{3,2,1,0:T(8,128)(2,1)} %all-gather.2.cloned.1.call-done), kind=kOutput, calls=%fused_computation.60 | convolution fusion | flops 402653184 | bytes 5341184 | tf_op jit(solution)/shard_map/dot_general | solution.py:44
  160.7 2.0 %fusion.36 = f32[4096,128]{1,0:T(8,128)S(1)} fusion(bf16[4096,384]{1,0:T(8,128)(2,1)S(1)} %bitcast.125, bf16[2,9,384,128]{3,2,1,0:T(8,128)(2,1)} %all-gather.2.cloned.1.call-done), kind=kOutput, calls=%fused_computation.62 | convolution fusion | flops 402653184 | bytes 5341184 | tf_op jit(solution)/shard_map/dot_general | solution.py:44
  162.7 1.9 %fusion.37 = f32[4096,128]{1,0:T(8,128)S(1)} fusion(bf16[4096,384]{1,0:T(8,128)(2,1)S(1)} %bitcast.123, bf16[2,9,384,128]{3,2,1,0:T(8,128)(2,1)} %all-gather.2.cloned.1.call-done), kind=kOutput, calls=%fused_computation.64 | convolution fusion | flops 402653184 | bytes 5341184 | tf_op jit(solution)/shard_map/dot_general | solution.py:44
  164.6 2.0 %fusion.38 = f32[4096,128]{1,0:T(8,128)S(1)} fusion(bf16[4096,384]{1,0:T(8,128)(2,1)S(1)} %bitcast.121, bf16[2,9,384,128]{3,2,1,0:T(8,128)(2,1)} %all-gather.2.cloned.1.call-done), kind=kOutput, calls=%fused_computation.66 | convolution fusion | flops 402653184 | bytes 5341184 | tf_op jit(solution)/shard_map/dot_general | solution.py:44
  166.7 2.5 %fusion.11 = f32[4096,128]{1,0:T(8,128)S(1)} fusion(f32[4096,128]{1,0:T(8,128)S(1)} %fusion.31, f32[4096,128]{1,0:T(8,128)S(1)} %fusion.32, f32[4096,128]{1,0:T(8,128)S(1)} %fusion.33, f32[4096,128]{1,0:T(8,128)S(1)} %fusion.34, f32[4096,128]{1,0:T(8,128)S(1)} %fusion.35, f32[4096,128]{1,0:T(8,128)S(1)} %fusion.36, f32[4096,128]{1,0:T(8,128)S(1)} %fusion.37, ...), kind=kOutput, calls=%fused_computation.17 | convolution fusion | flops 406847488 | bytes 22118400 | tf_op jit(solution)/shard_map/dot_general | solution.py:44
  169.1 1.3 add_convert_fusion
  (28 shorter events, 0.1 us)
Async XLA Ops:
  6.5 66.0 %all-gather.2.cloned.1.call-start = ((), (), s32[]{:S(2)}) async-start(), calls=%async_computation | async-start | bytes 2654208 | tf_op jit(solution)/shard_map/all_gather | solution.py:53
  8.3 25.9 %collective-permute-start = (bf16[2,4,512,128]{3,2,1,0:T(8,128)(2,1)S(1)}, bf16[2,4,512,128]{3,2,1,0:T(8,128)(2,1)S(1)}, u32[]{:S(2)}, u32[]{:S(2)}) collective-permute-start(bf16[2,4,512,128]{3,2,1,0:T(8,128)(2,1)S(1)} %fusion.24), channel_id=1, source_target_pairs={{0,4},{4,8},{8,12},{1,5},{5,9},{9,13},{2,6},{6,10},{10,14},{3,7},{... | collective-permute-start | bytes 3145736 | tf_op jit(solution)/shard_map/ppermute | solution.py:10
  35.3 11.0 %collective-permute-start.1 = (bf16[4,1,512,128]{3,2,1,0:T(8,128)(2,1)}, bf16[4,1,512,128]{3,2,1,0:T(8,128)(2,1)S(1)}, u32[]{:S(2)}, u32[]{:S(2)}) collective-permute-start(bf16[4,1,512,128]{3,2,1,0:T(8,128)(2,1)} %get-tuple-element.29), channel_id=1, source_target_pairs={{0,1},{1,2},{2,3},{4,5},{5,6},{6,7},{8,9},{9,10},{10,11},{12,13},{... | collective-permute-start | bytes 1572872 | tf_op jit(solution)/shard_map/ppermute | solution.py:21
  39.9 10.7 %collective-permute-start.2 = (bf16[4,1,512,128]{3,2,1,0:T(8,128)(2,1)}, bf16[4,1,512,128]{3,2,1,0:T(8,128)(2,1)S(1)}, u32[]{:S(2)}, u32[]{:S(2)}) collective-permute-start(bf16[4,1,512,128]{3,2,1,0:T(8,128)(2,1)} %get-tuple-element.30), channel_id=1, source_target_pairs={{1,0},{2,1},{3,2},{5,4},{6,5},{7,6},{9,8},{10,9},{11,10},{13,12},{... | collective-permute-start | bytes 1572872 | tf_op jit(solution)/shard_map/ppermute | solution.py:23
  72.5 3.0 %copy-start.7 = (bf16[2,4,512,384]{3,2,1,0:T(8,128)(2,1)S(1)}, bf16[2,4,512,384]{3,2,1,0:T(8,128)(2,1)}, u32[]{:S(2)}) copy-start(bf16[2,4,512,384]{3,2,1,0:T(8,128)(2,1)} %get-tuple-element.16) | copy-start | bytes 9437188
  75.6 2.0 %copy-start.5 = (bf16[2,4,512,384]{3,2,1,0:T(8,128)(2,1)S(1)}, bf16[2,4,512,384]{3,2,1,0:T(8,128)(2,1)}, u32[]{:S(2)}) copy-start(bf16[2,4,512,384]{3,2,1,0:T(8,128)(2,1)} %get-tuple-element.17) | copy-start | bytes 9437188
  77.6 2.0 %copy-start.3 = (bf16[2,4,512,384]{3,2,1,0:T(8,128)(2,1)S(1)}, bf16[2,4,512,384]{3,2,1,0:T(8,128)(2,1)}, u32[]{:S(2)}) copy-start(bf16[2,4,512,384]{3,2,1,0:T(8,128)(2,1)} %get-tuple-element.18) | copy-start | bytes 9437188
  79.6 2.0 %copy-start.2 = (bf16[2,4,512,384]{3,2,1,0:T(8,128)(2,1)S(1)}, bf16[2,4,512,384]{3,2,1,0:T(8,128)(2,1)}, u32[]{:S(2)}) copy-start(bf16[2,4,512,384]{3,2,1,0:T(8,128)(2,1)} %get-tuple-element.19) | copy-start | bytes 9437188
  81.7 2.0 %copy-start.1 = (bf16[2,4,512,384]{3,2,1,0:T(8,128)(2,1)S(1)}, bf16[2,4,512,384]{3,2,1,0:T(8,128)(2,1)}, u32[]{:S(2)}) copy-start(bf16[2,4,512,384]{3,2,1,0:T(8,128)(2,1)} %get-tuple-element.20) | copy-start | bytes 9437188
  83.8 2.0 %copy-start = (bf16[2,4,512,384]{3,2,1,0:T(8,128)(2,1)S(1)}, bf16[2,4,512,384]{3,2,1,0:T(8,128)(2,1)}, u32[]{:S(2)}) copy-start(bf16[2,4,512,384]{3,2,1,0:T(8,128)(2,1)} %get-tuple-element.21) | copy-start | bytes 9437188
  87.7 2.0 %copy-start.12 = (bf16[2,4,512,384]{3,2,1,0:T(8,128)(2,1)S(1)}, bf16[2,4,512,384]{3,2,1,0:T(8,128)(2,1)}, u32[]{:S(2)}) copy-start(bf16[2,4,512,384]{3,2,1,0:T(8,128)(2,1)} %get-tuple-element.14) | copy-start | bytes 9437188
  89.7 2.8 %copy-start.14 = (bf16[1,2,4,512,128]{4,3,2,1,0:T(8,128)(2,1)S(1)}, bf16[1,2,4,512,128]{4,3,2,1,0:T(8,128)(2,1)}, u32[]{:S(2)}) copy-start(bf16[1,2,4,512,128]{4,3,2,1,0:T(8,128)(2,1)} %param.2) | copy-start | bytes 3145732
  93.1 25.9 %collective-permute-start.3 = (bf16[2,4,512,128]{3,2,1,0:T(8,128)(2,1)S(1)}, bf16[2,4,512,128]{3,2,1,0:T(8,128)(2,1)S(1)}, u32[]{:S(2)}, u32[]{:S(2)}) collective-permute-start(bf16[2,4,512,128]{3,2,1,0:T(8,128)(2,1)S(1)} %fusion.30), channel_id=1, source_target_pairs={{0,4},{4,8},{8,12},{1,5},{5,9},{9,13},{2,6},{6,10},{10,14},{3,7},{... | collective-permute-start | bytes 3145736 | tf_op jit(solution)/shard_map/ppermute | solution.py:10
  119.2 10.6 %collective-permute-start.4 = (bf16[4,1,512,128]{3,2,1,0:T(8,128)(2,1)S(1)}, bf16[4,1,512,128]{3,2,1,0:T(8,128)(2,1)S(1)}, u32[]{:S(2)}, u32[]{:S(2)}) collective-permute-start(bf16[4,1,512,128]{3,2,1,0:T(8,128)(2,1)S(1)} %get-tuple-element.27), channel_id=1, source_target_pairs={{0,1},{1,2},{2,3},{4,5},{5,6},{6,7},{8,9},{9,10},{10,11},{12,13},{... | collective-permute-start | bytes 1572872 | tf_op jit(solution)/shard_map/ppermute | solution.py:21
  123.7 10.5 %collective-permute-start.5 = (bf16[4,1,512,128]{3,2,1,0:T(8,128)(2,1)S(1)}, bf16[4,1,512,128]{3,2,1,0:T(8,128)(2,1)S(1)}, u32[]{:S(2)}, u32[]{:S(2)}) collective-permute-start(bf16[4,1,512,128]{3,2,1,0:T(8,128)(2,1)S(1)} %get-tuple-element.28), channel_id=1, source_target_pairs={{1,0},{2,1},{3,2},{5,4},{6,5},{7,6},{9,8},{10,9},{11,10},{13,12},{... | collective-permute-start | bytes 1572872 | tf_op jit(solution)/shard_map/ppermute | solution.py:23
  149.5 3.0 %copy-start.11 = (bf16[2,4,512,384]{3,2,1,0:T(8,128)(2,1)S(1)}, bf16[2,4,512,384]{3,2,1,0:T(8,128)(2,1)}, u32[]{:S(2)}) copy-start(bf16[2,4,512,384]{3,2,1,0:T(8,128)(2,1)} %get-tuple-element.7) | copy-start | bytes 9437188
  152.5 2.0 %copy-start.10 = (bf16[2,4,512,384]{3,2,1,0:T(8,128)(2,1)S(1)}, bf16[2,4,512,384]{3,2,1,0:T(8,128)(2,1)}, u32[]{:S(2)}) copy-start(bf16[2,4,512,384]{3,2,1,0:T(8,128)(2,1)} %get-tuple-element.8) | copy-start | bytes 9437188
  154.6 2.0 %copy-start.9 = (bf16[2,4,512,384]{3,2,1,0:T(8,128)(2,1)S(1)}, bf16[2,4,512,384]{3,2,1,0:T(8,128)(2,1)}, u32[]{:S(2)}) copy-start(bf16[2,4,512,384]{3,2,1,0:T(8,128)(2,1)} %get-tuple-element.9) | copy-start | bytes 9437188
  156.6 2.0 %copy-start.8 = (bf16[2,4,512,384]{3,2,1,0:T(8,128)(2,1)S(1)}, bf16[2,4,512,384]{3,2,1,0:T(8,128)(2,1)}, u32[]{:S(2)}) copy-start(bf16[2,4,512,384]{3,2,1,0:T(8,128)(2,1)} %get-tuple-element.10) | copy-start | bytes 9437188
  158.6 2.0 %copy-start.6 = (bf16[2,4,512,384]{3,2,1,0:T(8,128)(2,1)S(1)}, bf16[2,4,512,384]{3,2,1,0:T(8,128)(2,1)}, u32[]{:S(2)}) copy-start(bf16[2,4,512,384]{3,2,1,0:T(8,128)(2,1)} %get-tuple-element.11) | copy-start | bytes 9437188
  160.7 2.0 %copy-start.4 = (bf16[2,4,512,384]{3,2,1,0:T(8,128)(2,1)S(1)}, bf16[2,4,512,384]{3,2,1,0:T(8,128)(2,1)}, u32[]{:S(2)}) copy-start(bf16[2,4,512,384]{3,2,1,0:T(8,128)(2,1)} %get-tuple-element.12) | copy-start | bytes 9437188
  164.6 2.0 %copy-start.13 = (bf16[2,4,512,384]{3,2,1,0:T(8,128)(2,1)S(1)}, bf16[2,4,512,384]{3,2,1,0:T(8,128)(2,1)}, u32[]{:S(2)}) copy-start(bf16[2,4,512,384]{3,2,1,0:T(8,128)(2,1)} %get-tuple-element.5) | copy-start | bytes 9437188
Sparse Core Ops, SparseCore 0:
  42.0 30.5 all-gather.1
where the time goes:
time: 178 us; the launch traced here: 177 us
  waiting for transfers between devices  69.6 us (39%)
  matrix products  39.3 us (22%)
  local copies, waits for them, and re-layouts  23.3 us (13%)
  starting transfers between devices  19.2 us (11%)
  between operations  13.9 us (8%)
  other arithmetic  12 us (7%)
    ppermute x2, waiting for transfers between devices, from_behind(): return lax.ppermute(block, axis, route)  45.5 us
    dot_general x18, matrix products, conv_block(): jnp.dot(slab.reshape(-1, 3 * chans), taps[time_tap * 3 + row_tap], prefer...  39.3 us
    slice x2, local copies, waits for them, and re-layouts, conv_block(): slab = joined[time_tap:time_tap + frames, row_tap:row_tap + rows]  18.6 us
    ppermute x2, starting transfers between devices, padded_2(): lax.ppermute(tail, axis, [(i, (i + 1) % count) for i in range(ends)])  9.08 us
    ppermute x2, waiting for transfers between devices, padded_2(): lax.ppermute(head, axis, [((i + 1) % count, i) for i in range(ends)])  8.69 us
    ppermute x2, waiting for transfers between devices, padded_2(): lax.ppermute(tail, axis, [(i, (i + 1) % count) for i in range(ends)])  8.64 us
    all_gather x1, waiting for transfers between devices, body(): all_taps = lax.all_gather(weights, 'section', axis=0, tiled=True)  6.69 us
    ppermute x2, starting transfers between devices, from_behind(): return lax.ppermute(block, axis, route)  6.32 us
  transfers between devices with their start and end apart: 7, of which 7 were waited for; matrix products, arithmetic and copies ran while one was open for 9% of the time, Pallas kernels for 0%

commit v1 on v0

--- a/solution.py
+++ b/solution.py
@@ -2,6 +2,7 @@
 import jax.numpy as jnp
 from jax import lax
 from jax.sharding import PartitionSpec as P
+from jax.lax import axis_index, ppermute, psum
 
 
 def from_behind(block, axis, distance):
@@ -50,7 +51,17 @@
 
 
 def body(video, weights):
-    all_taps = lax.all_gather(weights, "section", axis=0, tiled=True)
+    placed = psum(1, "section")
+    mixed_arr, all_values = (placed, axis_index("section"))
+    all_taps, passed = (weights, 1)
+    while passed < mixed_arr:
+        reached = ppermute(
+            all_taps, "section", tuple(((k0, k0 ^ passed) for k0 in range(mixed_arr)))
+        )
+        top = jnp.concatenate([all_taps, reached], axis=0)
+        x_now = jnp.concatenate([reached, all_taps], axis=0)
+        all_taps = jnp.where(all_values & passed == 0, top, x_now)
+        passed = 2 * passed
     first_taps = all_taps[0]
     second_taps = all_taps[1]
     index = 0

time: 178 us -> 153 us (0.86)
  waiting for transfers between devices: 69.6 us -> 52.5 us
  between operations: 13.9 us -> 0.52 us
  other arithmetic: 12 us -> 17.9 us
    ppermute x2, waiting for transfers between devices: 45.5 us -> 38.8 us  [from_behind(): return lax.ppermute(block, axis, route)]
    all_gather x1 -> x0, waiting for transfers between devices: 6.69 us -> none  [body(): all_taps = lax.all_gather(weights, 'section', axis=0, tiled=True)]
    select_n x0 -> x1, other arithmetic: none -> 3.56 us  [body(): all_taps = jnp.where(all_values & passed == 0, top, x_now)]
    ppermute x2, waiting for transfers between devices: 8.64 us -> 5.09 us  [padded_2(): lax.ppermute(tail, axis, [(i, (i + 1) % count) for i in range(ends)])]
    concatenate x2, other arithmetic: 3.45 us -> 5.67 us  [conv_block(): jnp.concatenate([padded[:, :, 0:width], padded[:, :, 1:width + 1], padded...]
  transfers between devices with their start and end apart: 7 -> 7, of which waited for: 7 -> 6; matrix products, arithmetic and copies ran while one was open for 9% -> 3% of each run, Pallas kernels for 0% -> 0%
where the time goes in v1:
time: 153 us; the launch traced here: 152 us
  waiting for transfers between devices  52.5 us (34%)
  matrix products  38.9 us (25%)
  local copies, waits for them, and re-layouts  22.5 us (15%)
  starting transfers between devices  19.8 us (13%)
  other arithmetic  17.9 us (12%)
    dot_general x18, matrix products, conv_block(): jnp.dot(slab.reshape(-1, 3 * chans), taps[time_tap * 3 + row_tap], prefer...  38.9 us
    ppermute x2, waiting for transfers between devices, from_behind(): return lax.ppermute(block, axis, route)  38.8 us
    slice x2, local copies, waits for them, and re-layouts, conv_block(): slab = joined[time_tap:time_tap + frames, row_tap:row_tap + rows]  17.8 us
    ppermute x2, waiting for transfers between devices, padded_2(): lax.ppermute(head, axis, [((i + 1) % count, i) for i in range(ends)])  8.68 us
    ppermute x2, starting transfers between devices, padded_2(): lax.ppermute(tail, axis, [(i, (i + 1) % count) for i in range(ends)])  8.25 us
    ppermute x2, starting transfers between devices, from_behind(): return lax.ppermute(block, axis, route)  6.41 us
    concatenate x2, other arithmetic, conv_block(): jnp.concatenate([padded[:, :, 0:width], padded[:, :, 1:width + 1], padded...  5.67 us
    ppermute x2, waiting for transfers between devices, padded_2(): lax.ppermute(tail, axis, [(i, (i + 1) % count) for i in range(ends)])  5.09 us
  transfers between devices with their start and end apart: 7, of which 6 were waited for; matrix products, arithmetic and copies ran while one was open for 3% of the time, Pallas kernels for 0%

profile of v1, /device:TPU:9, one launch (start us, length us, event | category | flops | bytes accessed | tf_op | source)
XLA Modules:
  0.0 152.1 jit_solution(8554043182278701610)
XLA Ops:
  0.0 1.8 %fusion.24 = bf16[2,4,512,128]{3,2,1,0:T(8,128)(2,1)S(1)} fusion(bf16[1,2,4,512,128]{4,3,2,1,0:T(8,128)(2,1)} %param.2), kind=kLoop, calls=%fused_computation.39 | loop fusion | flops 3145728 | bytes 2097152 | tf_op jit(solution)/shard_map/convert_element_type | solution.py:33
  1.8 0.0 copy-start.11
  1.8 3.2 %collective-permute-start = (bf16[2,4,512,128]{3,2,1,0:T(8,128)(2,1)S(1)}, bf16[2,4,512,128]{3,2,1,0:T(8,128)(2,1)S(1)}, u32[]{:S(2)}, u32[]{:S(2)}) collective-permute-start(bf16[2,4,512,128]{3,2,1,0:T(8,128)(2,1)S(1)} %fusion.24), channel_id=1, source_target_pairs={{0,4},{4,8},{8,12},{1,5},{5,9},{9,13},{2,6},{6,10},{10,14},{3,7},{... | collective-permute-start | bytes 3145736 | tf_op jit(solution)/shard_map/ppermute | solution.py:11
  5.0 1.3 collective-permute-start.3
  6.3 21.4 %collective-permute-done = bf16[2,4,512,128]{3,2,1,0:T(8,128)(2,1)S(1)} collective-permute-done((bf16[2,4,512,128]{3,2,1,0:T(8,128)(2,1)S(1)}, bf16[2,4,512,128]{3,2,1,0:T(8,128)(2,1)S(1)}, u32[]{:S(2)}, u32[]{:S(2)}) %collective-permute-start) | collective-permute-done | bytes 1048608 | tf_op jit(solution)/shard_map/ppermute | solution.py:11
  27.7 1.2 pad_maximum_fusion.5
  28.9 4.6 %collective-permute-start.1 = (bf16[4,1,512,128]{3,2,1,0:T(8,128)(2,1)}, bf16[4,1,512,128]{3,2,1,0:T(8,128)(2,1)S(1)}, u32[]{:S(2)}, u32[]{:S(2)}) collective-permute-start(bf16[4,1,512,128]{3,2,1,0:T(8,128)(2,1)} %get-tuple-element.29), channel_id=1, source_target_pairs={{0,1},{1,2},{2,3},{4,5},{5,6},{6,7},{8,9},{9,10},{10,11},{12,13},{... | collective-permute-start | bytes 1572872 | tf_op jit(solution)/shard_map/ppermute | solution.py:22
  33.5 1.9 %collective-permute-start.2 = (bf16[4,1,512,128]{3,2,1,0:T(8,128)(2,1)}, bf16[4,1,512,128]{3,2,1,0:T(8,128)(2,1)S(1)}, u32[]{:S(2)}, u32[]{:S(2)}) collective-permute-start(bf16[4,1,512,128]{3,2,1,0:T(8,128)(2,1)} %get-tuple-element.30), channel_id=1, source_target_pairs={{1,0},{2,1},{3,2},{5,4},{6,5},{7,6},{9,8},{10,9},{11,10},{13,12},{... | collective-permute-start | bytes 1572872 | tf_op jit(solution)/shard_map/ppermute | solution.py:24
  35.4 3.6 %maximum_select_fusion = bf16[2,9,384,128]{3,2,1,0:T(8,128)(2,1)} fusion(bf16[1,9,384,128]{3,2,1,0:T(8,128)(2,1)} %collective-permute-done.3, bf16[1,9,384,128]{3,2,1,0:T(8,128)(2,1)} %param.3, pred[]{:T(512)S(6)} %eq.3), kind=kLoop, calls=%fused_computation.47 | loop fusion | flops 2654208 | bytes 3538945 | tf_op jit(solution)/shard_map/jit(_where)/select_n | solution.py:63
  39.0 0.9 collective-permute-done.1
  39.9 4.3 %collective-permute-done.2 = bf16[4,1,512,128]{3,2,1,0:T(8,128)(2,1)S(1)} collective-permute-done((bf16[4,1,512,128]{3,2,1,0:T(8,128)(2,1)}, bf16[4,1,512,128]{3,2,1,0:T(8,128)(2,1)S(1)}, u32[]{:S(2)}, u32[]{:S(2)}) %collective-permute-start.2) | collective-permute-done | bytes 524320 | tf_op jit(solution)/shard_map/ppermute | solution.py:24
  44.2 1.9 %select_maximum_fusion.3 = bf16[4,6,514,128]{3,2,1,0:T(8,128)(2,1)S(1)} fusion(bf16[4,1,512,128]{3,2,1,0:T(8,128)(2,1)S(1)} %collective-permute-done.2, bf16[4,1,512,128]{3,2,1,0:T(8,128)(2,1)S(1)} %collective-permute-done.1, bf16[2,4,512,128]{3,2,1,0:T(8,128)(2,1)S(1)} %fusion.24, bf16[2,4,512,128]{3,2,1,0:T(8,128)(2,1)S(1)} %collective-permute-done), kind=kLoop, calls=%fused_computation.24 | loop fusion | flops 23685120 | bytes 6303744 | tf_op jit(solution)/shard_map/concatenate | solution.py:20
  46.1 0.0 copy-start.12
  46.1 2.3 %fusion.50 = (bf16[4,6,512,128]{3,2,1,0:T(8,128)(2,1)S(1)}, bf16[4,6,512,128]{3,2,1,0:T(8,128)(2,1)S(1)}) fusion(bf16[4,6,514,128]{3,2,1,0:T(8,128)(2,1)S(1)} %select_maximum_fusion.3), kind=kLoop, calls=%fused_computation.89 | loop fusion | bytes 12582912 | tf_op jit(solution)/shard_map/slice | solution.py:39
  48.4 3.9 %pad_maximum_fusion = bf16[4,6,512,384]{3,2,1,0:T(8,128)(2,1)S(1)} fusion(bf16[4,6,512,128]{3,2,1,0:T(8,128)(2,1)S(1)} %get-tuple-element.26, bf16[4,1,512,128]{3,2,1,0:T(8,128)(2,1)} %copy-done.19, bf16[2,4,512,128]{3,2,1,0:T(8,128)(2,1)S(1)} %copy-done.12, bf16[2,4,512,128]{3,2,1,0:T(8,128)(2,1)S(1)} %copy-done.16, bf16[4,1,512,128]{3,2,1,0:T(8,128)(2,1)} %copy-done.18, ...), kind=kLoop, calls=%fused_computation.2 | loop fusion | flops 56623104 | bytes 18874368 | tf_op jit(solution)/shard_map/concatenate | solution.py:38
  52.4 8.4 %fusion.48 = (bf16[2,4,512,384]{3,2,1,0:T(8,128)(2,1)}, bf16[2,4,512,384]{3,2,1,0:T(8,128)(2,1)}, bf16[2,4,512,384]{3,2,1,0:T(8,128)(2,1)}, bf16[2,4,512,384]{3,...) fusion(bf16[4,6,512,384]{3,2,1,0:T(8,128)(2,1)S(1)} %pad_maximu, ...), kind=kLoop, calls=%fused_computation.87 | loop fusion | bytes 56623104 | tf_op jit(solution)/shard_map/slice | solution.py:44
  60.8 3.0 %fusion.39 = f32[4096,128]{1,0:T(8,128)S(1)} fusion(bf16[4096,384]{1,0:T(8,128)(2,1)} %bitcast.131, bf16[2,9,384,128]{3,2,1,0:T(8,128)(2,1)} %maximum_select_fusion), kind=kOutput, calls=%fused_computation.70 | convolution fusion | flops 402653184 | bytes 5341184 | tf_op jit(solution)/shard_map/dot_general | solution.py:45
  63.9 2.0 %fusion.40 = f32[4096,128]{1,0:T(8,128)S(1)} fusion(bf16[4096,384]{1,0:T(8,128)(2,1)S(1)} %bitcast.129, bf16[2,9,384,128]{3,2,1,0:T(8,128)(2,1)} %maximum_select_fusion), kind=kOutput, calls=%fused_computation.72 | convolution fusion | flops 402653184 | bytes 5341184 | tf_op jit(solution)/shard_map/dot_general | solution.py:45
  65.9 2.0 %fusion.41 = f32[4096,128]{1,0:T(8,128)S(1)} fusion(bf16[4096,384]{1,0:T(8,128)(2,1)S(1)} %bitcast.127, bf16[2,9,384,128]{3,2,1,0:T(8,128)(2,1)} %maximum_select_fusion), kind=kOutput, calls=%fused_computation.74 | convolution fusion | flops 402653184 | bytes 5341184 | tf_op jit(solution)/shard_map/dot_general | solution.py:45
  68.0 2.0 %fusion.42 = f32[4096,128]{1,0:T(8,128)S(1)} fusion(bf16[4096,384]{1,0:T(8,128)(2,1)S(1)} %bitcast.125, bf16[2,9,384,128]{3,2,1,0:T(8,128)(2,1)} %maximum_select_fusion), kind=kOutput, calls=%fused_computation.76 | convolution fusion | flops 402653184 | bytes 5341184 | tf_op jit(solution)/shard_map/dot_general | solution.py:45
  70.0 2.0 %fusion.43 = f32[4096,128]{1,0:T(8,128)S(1)} fusion(bf16[4096,384]{1,0:T(8,128)(2,1)S(1)} %bitcast.123, bf16[2,9,384,128]{3,2,1,0:T(8,128)(2,1)} %maximum_select_fusion), kind=kOutput, calls=%fused_computation.78 | convolution fusion | flops 402653184 | bytes 5341184 | tf_op jit(solution)/shard_map/dot_general | solution.py:45
  72.1 1.9 %fusion.44 = f32[4096,128]{1,0:T(8,128)S(1)} fusion(bf16[4096,384]{1,0:T(8,128)(2,1)S(1)} %bitcast.121, bf16[2,9,384,128]{3,2,1,0:T(8,128)(2,1)} %maximum_select_fusion), kind=kOutput, calls=%fused_computation.80 | convolution fusion | flops 402653184 | bytes 5341184 | tf_op jit(solution)/shard_map/dot_general | solution.py:45
  74.0 1.9 %fusion.45 = f32[4096,128]{1,0:T(8,128)S(1)} fusion(bf16[4096,384]{1,0:T(8,128)(2,1)S(1)} %bitcast.119, bf16[2,9,384,128]{3,2,1,0:T(8,128)(2,1)} %maximum_select_fusion), kind=kOutput, calls=%fused_computation.82 | convolution fusion | flops 402653184 | bytes 5341184 | tf_op jit(solution)/shard_map/dot_general | solution.py:45
  75.9 2.0 %fusion.46 = f32[4096,128]{1,0:T(8,128)S(1)} fusion(bf16[4096,384]{1,0:T(8,128)(2,1)S(1)} %bitcast.117, bf16[2,9,384,128]{3,2,1,0:T(8,128)(2,1)} %maximum_select_fusion), kind=kOutput, calls=%fused_computation.84 | convolution fusion | flops 402653184 | bytes 5341184 | tf_op jit(solution)/shard_map/dot_general | solution.py:45
  77.9 0.0 copy-start.17
  77.9 2.6 %fusion.14 = f32[4096,128]{1,0:T(8,128)S(1)} fusion(f32[4096,128]{1,0:T(8,128)S(1)} %fusion.39, f32[4096,128]{1,0:T(8,128)S(1)} %fusion.40, f32[4096,128]{1,0:T(8,128)S(1)} %fusion.41, f32[4096,128]{1,0:T(8,128)S(1)} %fusion.42, f32[4096,128]{1,0:T(8,128)S(1)} %fusion.43, f32[4096,128]{1,0:T(8,128)S(1)} %fusion.44, f32[4096,128]{1,0:T(8,128)S(1)} %fusion.45, ...), kind=kOutput, calls=%fused_computation.20 | convolution fusion | flops 406847488 | bytes 22118400 | tf_op jit(solution)/shard_map/dot_general | solution.py:45
  80.5 0.6 fusion.30
  81.0 3.2 %collective-permute-start.4 = (bf16[2,4,512,128]{3,2,1,0:T(8,128)(2,1)S(1)}, bf16[2,4,512,128]{3,2,1,0:T(8,128)(2,1)S(1)}, u32[]{:S(2)}, u32[]{:S(2)}) collective-permute-start(bf16[2,4,512,128]{3,2,1,0:T(8,128)(2,1)S(1)} %fusion.30), channel_id=1, source_target_pairs={{0,4},{4,8},{8,12},{1,5},{5,9},{9,13},{2,6},{6,10},{10,14},{3,7},{... | collective-permute-start | bytes 3145736 | tf_op jit(solution)/shard_map/ppermute | solution.py:11
  84.3 17.3 %collective-permute-done.4 = bf16[2,4,512,128]{3,2,1,0:T(8,128)(2,1)S(1)} collective-permute-done((bf16[2,4,512,128]{3,2,1,0:T(8,128)(2,1)S(1)}, bf16[2,4,512,128]{3,2,1,0:T(8,128)(2,1)S(1)}, u32[]{:S(2)}, u32[]{:S(2)}) %collective-permute-start.4) | collective-permute-done | bytes 1048608 | tf_op jit(solution)/shard_map/ppermute | solution.py:11
  101.6 0.1 pad_maximum_fusion.3
  101.7 3.7 %collective-permute-start.5 = (bf16[4,1,512,128]{3,2,1,0:T(8,128)(2,1)S(1)}, bf16[4,1,512,128]{3,2,1,0:T(8,128)(2,1)S(1)}, u32[]{:S(2)}, u32[]{:S(2)}) collective-permute-start(bf16[4,1,512,128]{3,2,1,0:T(8,128)(2,1)S(1)} %get-tuple-element.27), channel_id=1, source_target_pairs={{0,1},{1,2},{2,3},{4,5},{5,6},{6,7},{8,9},{9,10},{10,11},{12,13},{... | collective-permute-start | bytes 1572872 | tf_op jit(solution)/shard_map/ppermute | solution.py:22
  105.4 1.9 %collective-permute-start.6 = (bf16[4,1,512,128]{3,2,1,0:T(8,128)(2,1)S(1)}, bf16[4,1,512,128]{3,2,1,0:T(8,128)(2,1)S(1)}, u32[]{:S(2)}, u32[]{:S(2)}) collective-permute-start(bf16[4,1,512,128]{3,2,1,0:T(8,128)(2,1)S(1)} %get-tuple-element.28), channel_id=1, source_target_pairs={{1,0},{2,1},{3,2},{5,4},{6,5},{7,6},{9,8},{10,9},{11,10},{13,12},{... | collective-permute-start | bytes 1572872 | tf_op jit(solution)/shard_map/ppermute | solution.py:24
  107.3 4.2 %collective-permute-done.5 = bf16[4,1,512,128]{3,2,1,0:T(8,128)(2,1)S(1)} collective-permute-done((bf16[4,1,512,128]{3,2,1,0:T(8,128)(2,1)S(1)}, bf16[4,1,512,128]{3,2,1,0:T(8,128)(2,1)S(1)}, u32[]{:S(2)}, u32[]{:S(2)}) %collective-permute-start.5) | collective-permute-done | bytes 524320 | tf_op jit(solution)/shard_map/ppermute | solution.py:22
  111.5 4.4 %collective-permute-done.6 = bf16[4,1,512,128]{3,2,1,0:T(8,128)(2,1)S(1)} collective-permute-done((bf16[4,1,512,128]{3,2,1,0:T(8,128)(2,1)S(1)}, bf16[4,1,512,128]{3,2,1,0:T(8,128)(2,1)S(1)}, u32[]{:S(2)}, u32[]{:S(2)}) %collective-permute-start.6) | collective-permute-done | bytes 524320 | tf_op jit(solution)/shard_map/ppermute | solution.py:24
  115.9 1.9 %select_maximum_fusion = bf16[4,6,514,128]{3,2,1,0:T(8,128)(2,1)S(1)} fusion(bf16[4,1,512,128]{3,2,1,0:T(8,128)(2,1)S(1)} %collective-permute-done.6, bf16[4,1,512,128]{3,2,1,0:T(8,128)(2,1)S(1)} %collective-permute-done.5, bf16[2,4,512,128]{3,2,1,0:T(8,128)(2,1)S(1)} %fusion.30, bf16[2,4,512,128]{3,2,1,0:T(8,128)(2,1)S(1)} %collective-permute-done.4), kind=kLoop, calls=%fused_computation.21 | loop fusion | flops 23685120 | bytes 6303744 | tf_op jit(solution)/shard_map/concatenate | solution.py:20
  117.8 2.3 %fusion.49 = (bf16[4,6,512,128]{3,2,1,0:T(8,128)(2,1)S(1)}, bf16[4,6,512,128]{3,2,1,0:T(8,128)(2,1)S(1)}) fusion(bf16[4,6,514,128]{3,2,1,0:T(8,128)(2,1)S(1)} %select_maximum_fusion), kind=kLoop, calls=%fused_computation.88 | loop fusion | bytes 12582912 | tf_op jit(solution)/shard_map/slice | solution.py:39
  120.1 1.7 %pad_maximum_fusion.1 = bf16[4,6,512,384]{3,2,1,0:T(8,128)(2,1)S(1)} fusion(bf16[4,6,512,128]{3,2,1,0:T(8,128)(2,1)S(1)} %get-tuple-element.24, bf16[4,1,512,128]{3,2,1,0:T(8,128)(2,1)S(1)} %collective-permute-done.6, bf16[2,4,512,128]{3,2,1,0:T(8,128)(2,1)S(1)} %fusion.30, bf16[2,4,512,128]{3,2,1,0:T(8,128)(2,1)S(1)} %collective-permute-done.4, ...), kind=kLoop, calls=%fused_computation.3 | loop fusion | flops 56623104 | bytes 18874368 | tf_op jit(solution)/shard_map/concatenate | solution.py:38
  121.8 9.3 %fusion.47 = (bf16[2,4,512,384]{3,2,1,0:T(8,128)(2,1)}, bf16[2,4,512,384]{3,2,1,0:T(8,128)(2,1)}, bf16[2,4,512,384]{3,2,1,0:T(8,128)(2,1)}, bf16[2,4,512,384]{3,...) fusion(bf16[4,6,512,384]{3,2,1,0:T(8,128)(2,1)S(1)} %pad_maximu, ...), kind=kLoop, calls=%fused_computation.86 | loop fusion | bytes 56623104 | tf_op jit(solution)/shard_map/slice | solution.py:44
  131.2 3.0 %fusion.31 = f32[4096,128]{1,0:T(8,128)S(1)} fusion(bf16[4096,384]{1,0:T(8,128)(2,1)} %bitcast.132, bf16[2,9,384,128]{3,2,1,0:T(8,128)(2,1)} %maximum_select_fusion), kind=kOutput, calls=%fused_computation.53 | convolution fusion | flops 402653184 | bytes 5341184 | tf_op jit(solution)/shard_map/dot_general | solution.py:45
  134.2 2.0 %fusion.32 = f32[4096,128]{1,0:T(8,128)S(1)} fusion(bf16[4096,384]{1,0:T(8,128)(2,1)S(1)} %bitcast.130, bf16[2,9,384,128]{3,2,1,0:T(8,128)(2,1)} %maximum_select_fusion), kind=kOutput, calls=%fused_computation.55 | convolution fusion | flops 402653184 | bytes 5341184 | tf_op jit(solution)/shard_map/dot_general | solution.py:45
  136.2 2.0 %fusion.33 = f32[4096,128]{1,0:T(8,128)S(1)} fusion(bf16[4096,384]{1,0:T(8,128)(2,1)S(1)} %bitcast.128, bf16[2,9,384,128]{3,2,1,0:T(8,128)(2,1)} %maximum_select_fusion), kind=kOutput, calls=%fused_computation.57 | convolution fusion | flops 402653184 | bytes 5341184 | tf_op jit(solution)/shard_map/dot_general | solution.py:45
  138.3 2.0 %fusion.34 = f32[4096,128]{1,0:T(8,128)S(1)} fusion(bf16[4096,384]{1,0:T(8,128)(2,1)S(1)} %bitcast.126, bf16[2,9,384,128]{3,2,1,0:T(8,128)(2,1)} %maximum_select_fusion), kind=kOutput, calls=%fused_computation.59 | convolution fusion | flops 402653184 | bytes 5341184 | tf_op jit(solution)/shard_map/dot_general | solution.py:45
  140.3 2.0 %fusion.35 = f32[4096,128]{1,0:T(8,128)S(1)} fusion(bf16[4096,384]{1,0:T(8,128)(2,1)S(1)} %bitcast.124, bf16[2,9,384,128]{3,2,1,0:T(8,128)(2,1)} %maximum_select_fusion), kind=kOutput, calls=%fused_computation.61 | convolution fusion | flops 402653184 | bytes 5341184 | tf_op jit(solution)/shard_map/dot_general | solution.py:45
  142.4 2.0 %fusion.36 = f32[4096,128]{1,0:T(8,128)S(1)} fusion(bf16[4096,384]{1,0:T(8,128)(2,1)S(1)} %bitcast.122, bf16[2,9,384,128]{3,2,1,0:T(8,128)(2,1)} %maximum_select_fusion), kind=kOutput, calls=%fused_computation.63 | convolution fusion | flops 402653184 | bytes 5341184 | tf_op jit(solution)/shard_map/dot_general | solution.py:45
  144.4 1.9 %fusion.37 = f32[4096,128]{1,0:T(8,128)S(1)} fusion(bf16[4096,384]{1,0:T(8,128)(2,1)S(1)} %bitcast.120, bf16[2,9,384,128]{3,2,1,0:T(8,128)(2,1)} %maximum_select_fusion), kind=kOutput, calls=%fused_computation.65 | convolution fusion | flops 402653184 | bytes 5341184 | tf_op jit(solution)/shard_map/dot_general | solution.py:45
  146.3 2.0 %fusion.38 = f32[4096,128]{1,0:T(8,128)S(1)} fusion(bf16[4096,384]{1,0:T(8,128)(2,1)S(1)} %bitcast.118, bf16[2,9,384,128]{3,2,1,0:T(8,128)(2,1)} %maximum_select_fusion), kind=kOutput, calls=%fused_computation.67 | convolution fusion | flops 402653184 | bytes 5341184 | tf_op jit(solution)/shard_map/dot_general | solution.py:45
  148.4 2.5 %fusion.11 = f32[4096,128]{1,0:T(8,128)S(1)} fusion(f32[4096,128]{1,0:T(8,128)S(1)} %fusion.31, f32[4096,128]{1,0:T(8,128)S(1)} %fusion.32, f32[4096,128]{1,0:T(8,128)S(1)} %fusion.33, f32[4096,128]{1,0:T(8,128)S(1)} %fusion.34, f32[4096,128]{1,0:T(8,128)S(1)} %fusion.35, f32[4096,128]{1,0:T(8,128)S(1)} %fusion.36, f32[4096,128]{1,0:T(8,128)S(1)} %fusion.37, ...), kind=kOutput, calls=%fused_computation.17 | convolution fusion | flops 406847488 | bytes 22118400 | tf_op jit(solution)/shard_map/dot_general | solution.py:45
  150.8 1.3 add_convert_fusion
  (38 shorter events, 0.1 us)
Async XLA Ops:
  1.8 42.4 %copy-start.11 = (bf16[2,4,512,128]{3,2,1,0:T(8,128)(2,1)}, bf16[2,4,512,128]{3,2,1,0:T(8,128)(2,1)S(1)}, u32[]{:S(2)}) copy-start(bf16[2,4,512,128]{3,2,1,0:T(8,128)(2,1)S(1)} %fusion.24) | copy-start | bytes 3145732
  1.8 25.9 %collective-permute-start = (bf16[2,4,512,128]{3,2,1,0:T(8,128)(2,1)S(1)}, bf16[2,4,512,128]{3,2,1,0:T(8,128)(2,1)S(1)}, u32[]{:S(2)}, u32[]{:S(2)}) collective-permute-start(bf16[2,4,512,128]{3,2,1,0:T(8,128)(2,1)S(1)} %fusion.24), channel_id=1, source_target_pairs={{0,4},{4,8},{8,12},{1,5},{5,9},{9,13},{2,6},{6,10},{10,14},{3,7},{... | collective-permute-start | bytes 3145736 | tf_op jit(solution)/shard_map/ppermute | solution.py:11
  5.0 30.4 %collective-permute-start.3 = (bf16[1,9,384,128]{3,2,1,0:T(8,128)(2,1)}, bf16[1,9,384,128]{3,2,1,0:T(8,128)(2,1)}, u32[]{:S(2)}, u32[]{:S(2)}) collective-permute-start(bf16[1,9,384,128]{3,2,1,0:T(8,128)(2,1)} %param.3), channel_id=1, source_target_pairs={{0,16},{16,0},{1,17},{17,1},{2,18},{18,2},{3,19},{19,3},{4,20},{20... | collective-permute-start | bytes 2654216 | tf_op jit(solution)/shard_map/ppermute | solution.py:58
  27.7 16.5 %copy-start.15 = (bf16[2,4,512,128]{3,2,1,0:T(8,128)(2,1)}, bf16[2,4,512,128]{3,2,1,0:T(8,128)(2,1)S(1)}, u32[]{:S(2)}) copy-start(bf16[2,4,512,128]{3,2,1,0:T(8,128)(2,1)S(1)} %collective-permute-done) | copy-start | bytes 3145732
  28.9 11.0 %collective-permute-start.1 = (bf16[4,1,512,128]{3,2,1,0:T(8,128)(2,1)}, bf16[4,1,512,128]{3,2,1,0:T(8,128)(2,1)S(1)}, u32[]{:S(2)}, u32[]{:S(2)}) collective-permute-start(bf16[4,1,512,128]{3,2,1,0:T(8,128)(2,1)} %get-tuple-element.29), channel_id=1, source_target_pairs={{0,1},{1,2},{2,3},{4,5},{5,6},{6,7},{8,9},{9,10},{10,11},{12,13},{... | collective-permute-start | bytes 1572872 | tf_op jit(solution)/shard_map/ppermute | solution.py:22
  33.5 10.7 %collective-permute-start.2 = (bf16[4,1,512,128]{3,2,1,0:T(8,128)(2,1)}, bf16[4,1,512,128]{3,2,1,0:T(8,128)(2,1)S(1)}, u32[]{:S(2)}, u32[]{:S(2)}) collective-permute-start(bf16[4,1,512,128]{3,2,1,0:T(8,128)(2,1)} %get-tuple-element.30), channel_id=1, source_target_pairs={{1,0},{2,1},{3,2},{5,4},{6,5},{7,6},{9,8},{10,9},{11,10},{13,12},{... | collective-permute-start | bytes 1572872 | tf_op jit(solution)/shard_map/ppermute | solution.py:24
  39.9 6.2 %copy-start.18 = (bf16[4,1,512,128]{3,2,1,0:T(8,128)(2,1)}, bf16[4,1,512,128]{3,2,1,0:T(8,128)(2,1)S(1)}, u32[]{:S(2)}) copy-start(bf16[4,1,512,128]{3,2,1,0:T(8,128)(2,1)S(1)} %collective-permute-done.1) | copy-start | bytes 1572868
  44.2 1.9 %copy-start.19 = (bf16[4,1,512,128]{3,2,1,0:T(8,128)(2,1)}, bf16[4,1,512,128]{3,2,1,0:T(8,128)(2,1)S(1)}, u32[]{:S(2)}) copy-start(bf16[4,1,512,128]{3,2,1,0:T(8,128)(2,1)S(1)} %collective-permute-done.2) | copy-start | bytes 1572868
  46.1 2.3 %copy-start.12 = (bf16[2,4,512,128]{3,2,1,0:T(8,128)(2,1)S(1)}, bf16[2,4,512,128]{3,2,1,0:T(8,128)(2,1)}, u32[]{:S(2)}) copy-start(bf16[2,4,512,128]{3,2,1,0:T(8,128)(2,1)} %copy-done.11) | copy-start | bytes 3145732
  46.1 2.3 %copy-start.16 = (bf16[2,4,512,128]{3,2,1,0:T(8,128)(2,1)S(1)}, bf16[2,4,512,128]{3,2,1,0:T(8,128)(2,1)}, u32[]{:S(2)}) copy-start(bf16[2,4,512,128]{3,2,1,0:T(8,128)(2,1)} %copy-done.15) | copy-start | bytes 3145732
  60.8 3.0 %copy-start.9 = (bf16[2,4,512,384]{3,2,1,0:T(8,128)(2,1)S(1)}, bf16[2,4,512,384]{3,2,1,0:T(8,128)(2,1)}, u32[]{:S(2)}) copy-start(bf16[2,4,512,384]{3,2,1,0:T(8,128)(2,1)} %get-tuple-element.16) | copy-start | bytes 9437188
  63.9 2.0 %copy-start.7 = (bf16[2,4,512,384]{3,2,1,0:T(8,128)(2,1)S(1)}, bf16[2,4,512,384]{3,2,1,0:T(8,128)(2,1)}, u32[]{:S(2)}) copy-start(bf16[2,4,512,384]{3,2,1,0:T(8,128)(2,1)} %get-tuple-element.17) | copy-start | bytes 9437188
  65.9 2.0 %copy-start.5 = (bf16[2,4,512,384]{3,2,1,0:T(8,128)(2,1)S(1)}, bf16[2,4,512,384]{3,2,1,0:T(8,128)(2,1)}, u32[]{:S(2)}) copy-start(bf16[2,4,512,384]{3,2,1,0:T(8,128)(2,1)} %get-tuple-element.18) | copy-start | bytes 9437188
  68.0 2.0 %copy-start.3 = (bf16[2,4,512,384]{3,2,1,0:T(8,128)(2,1)S(1)}, bf16[2,4,512,384]{3,2,1,0:T(8,128)(2,1)}, u32[]{:S(2)}) copy-start(bf16[2,4,512,384]{3,2,1,0:T(8,128)(2,1)} %get-tuple-element.19) | copy-start | bytes 9437188
  70.0 2.0 %copy-start.1 = (bf16[2,4,512,384]{3,2,1,0:T(8,128)(2,1)S(1)}, bf16[2,4,512,384]{3,2,1,0:T(8,128)(2,1)}, u32[]{:S(2)}) copy-start(bf16[2,4,512,384]{3,2,1,0:T(8,128)(2,1)} %get-tuple-element.20) | copy-start | bytes 9437188
  75.8 2.0 %copy-start.14 = (bf16[2,4,512,384]{3,2,1,0:T(8,128)(2,1)S(1)}, bf16[2,4,512,384]{3,2,1,0:T(8,128)(2,1)}, u32[]{:S(2)}) copy-start(bf16[2,4,512,384]{3,2,1,0:T(8,128)(2,1)} %get-tuple-element.14) | copy-start | bytes 9437188
  77.9 2.6 %copy-start.17 = (bf16[1,2,4,512,128]{4,3,2,1,0:T(8,128)(2,1)S(1)}, bf16[1,2,4,512,128]{4,3,2,1,0:T(8,128)(2,1)}, u32[]{:S(2)}) copy-start(bf16[1,2,4,512,128]{4,3,2,1,0:T(8,128)(2,1)} %param.2) | copy-start | bytes 3145732
  81.0 20.6 %collective-permute-start.4 = (bf16[2,4,512,128]{3,2,1,0:T(8,128)(2,1)S(1)}, bf16[2,4,512,128]{3,2,1,0:T(8,128)(2,1)S(1)}, u32[]{:S(2)}, u32[]{:S(2)}) collective-permute-start(bf16[2,4,512,128]{3,2,1,0:T(8,128)(2,1)S(1)} %fusion.30), channel_id=1, source_target_pairs={{0,4},{4,8},{8,12},{1,5},{5,9},{9,13},{2,6},{6,10},{10,14},{3,7},{... | collective-permute-start | bytes 3145736 | tf_op jit(solution)/shard_map/ppermute | solution.py:11
  101.7 9.8 %collective-permute-start.5 = (bf16[4,1,512,128]{3,2,1,0:T(8,128)(2,1)S(1)}, bf16[4,1,512,128]{3,2,1,0:T(8,128)(2,1)S(1)}, u32[]{:S(2)}, u32[]{:S(2)}) collective-permute-start(bf16[4,1,512,128]{3,2,1,0:T(8,128)(2,1)S(1)} %get-tuple-element.27), channel_id=1, source_target_pairs={{0,1},{1,2},{2,3},{4,5},{5,6},{6,7},{8,9},{9,10},{10,11},{12,13},{... | collective-permute-start | bytes 1572872 | tf_op jit(solution)/shard_map/ppermute | solution.py:22
  105.4 10.5 %collective-permute-start.6 = (bf16[4,1,512,128]{3,2,1,0:T(8,128)(2,1)S(1)}, bf16[4,1,512,128]{3,2,1,0:T(8,128)(2,1)S(1)}, u32[]{:S(2)}, u32[]{:S(2)}) collective-permute-start(bf16[4,1,512,128]{3,2,1,0:T(8,128)(2,1)S(1)} %get-tuple-element.28), channel_id=1, source_target_pairs={{1,0},{2,1},{3,2},{5,4},{6,5},{7,6},{9,8},{10,9},{11,10},{13,12},{... | collective-permute-start | bytes 1572872 | tf_op jit(solution)/shard_map/ppermute | solution.py:24
  131.2 3.0 %copy-start.10 = (bf16[2,4,512,384]{3,2,1,0:T(8,128)(2,1)S(1)}, bf16[2,4,512,384]{3,2,1,0:T(8,128)(2,1)}, u32[]{:S(2)}) copy-start(bf16[2,4,512,384]{3,2,1,0:T(8,128)(2,1)} %get-tuple-element.7) | copy-start | bytes 9437188
  134.2 2.0 %copy-start.8 = (bf16[2,4,512,384]{3,2,1,0:T(8,128)(2,1)S(1)}, bf16[2,4,512,384]{3,2,1,0:T(8,128)(2,1)}, u32[]{:S(2)}) copy-start(bf16[2,4,512,384]{3,2,1,0:T(8,128)(2,1)} %get-tuple-element.8) | copy-start | bytes 9437188
  136.2 2.0 %copy-start.6 = (bf16[2,4,512,384]{3,2,1,0:T(8,128)(2,1)S(1)}, bf16[2,4,512,384]{3,2,1,0:T(8,128)(2,1)}, u32[]{:S(2)}) copy-start(bf16[2,4,512,384]{3,2,1,0:T(8,128)(2,1)} %get-tuple-element.9) | copy-start | bytes 9437188
  138.3 2.0 %copy-start.4 = (bf16[2,4,512,384]{3,2,1,0:T(8,128)(2,1)S(1)}, bf16[2,4,512,384]{3,2,1,0:T(8,128)(2,1)}, u32[]{:S(2)}) copy-start(bf16[2,4,512,384]{3,2,1,0:T(8,128)(2,1)} %get-tuple-element.10) | copy-start | bytes 9437188
  140.3 2.0 %copy-start.2 = (bf16[2,4,512,384]{3,2,1,0:T(8,128)(2,1)S(1)}, bf16[2,4,512,384]{3,2,1,0:T(8,128)(2,1)}, u32[]{:S(2)}) copy-start(bf16[2,4,512,384]{3,2,1,0:T(8,128)(2,1)} %get-tuple-element.11) | copy-start | bytes 9437188
  142.4 2.0 %copy-start = (bf16[2,4,512,384]{3,2,1,0:T(8,128)(2,1)S(1)}, bf16[2,4,512,384]{3,2,1,0:T(8,128)(2,1)}, u32[]{:S(2)}) copy-start(bf16[2,4,512,384]{3,2,1,0:T(8,128)(2,1)} %get-tuple-element.12) | copy-start | bytes 9437188
  146.3 2.1 %copy-start.13 = (bf16[2,4,512,384]{3,2,1,0:T(8,128)(2,1)S(1)}, bf16[2,4,512,384]{3,2,1,0:T(8,128)(2,1)}, u32[]{:S(2)}) copy-start(bf16[2,4,512,384]{3,2,1,0:T(8,128)(2,1)} %get-tuple-element.5) | copy-start | bytes 9437188
